TPU v7x, 512 devices: a whole 4x8x8 slice. The times are simulated.
512 devices in a mesh: dp: 32 (over y, x), section: 4 (over z_hi), space: 4 (over z_lo, core).
Axes of the slice: x: 4, y: 8, z: 8 (z_hi: 4, z_lo: 2; z = z_hi * 2 + z_lo), core: 2. Of those that a mesh axis runs over, the one named last changes fastest.
Arguments:
- images: bfloat16 [64, 4, 64, 256], P('dp', 'space'), may hold values from -6 to 6
- steps: int32 [64], P('dp'), may hold values from 0 to 999
- out_grad: bfloat16 [64, 4, 64, 256], P('dp', 'space'), may hold values from -0.125 to 0.125
- conv_weight: bfloat16 [4, 3, 3, 256, 256], P('section'), may hold values from -0.125 to 0.125
- gn_gain: float32 [4, 256], P('section'), may hold values from 0.5 to 2
- emb_weight: bfloat16 [4, 256, 512], P('section'), may hold values from -0.375 to 0.375
Outputs:
- grad_conv: float32 [4, 3, 3, 256, 256], P('section')
- grad_gain: float32 [4, 256], P('section')
- grad_emb: float32 [4, 256, 512], P('section')
All inputs are finite; a program needn't handle non-finite values.
Results may differ from a plain program's by a relative error of at most 0.0064.
Values may be sent and summed in bfloat16 or wider, within the bound.
No kernel may reach another device: no remote copies, remote signals or barrier semaphores. Data moves between devices by JAX's collectives and lax.ppermute only.
A program may use at most 64 MiB of HBM per device.

v0:
```python
import math
import jax
import jax.numpy as jnp
from jax import lax
from jax.sharding import PartitionSpec as P

G = 32
FREQ = 256
MICRO = 2
EPS = 1e-05


def from_behind(value, axis, steps):
    count = lax.axis_size(axis)
    initial, last = (max(0, -steps), min(count, count - steps))
    return lax.ppermute(value, axis, [(source, source + steps) for source in range(initial, last)])


def extended(shard, sides, width):
    for axis, dim in sides:
        size, length = (lax.axis_size(axis), shard.shape[dim])
        up = [(i, (i + 1) % size) for i in range(size - 1)]
        down = [(j, i) for i, j in up]
        last = lax.slice_in_dim(shard, length - width, length, axis=dim)
        initial = lax.slice_in_dim(shard, 0, width, axis=dim)
        before = lax.ppermute(last, axis, up)
        after = lax.ppermute(initial, axis, down)
        shard = jnp.concatenate([before, shard, after], axis=dim)
    return shard


def sinusoid(timesteps, feature_n):
    half_n = feature_n // 2
    freqs = jnp.exp(-math.log(10000.0) * jnp.arange(half_n, dtype=jnp.float32) / half_n)
    angles = timesteps.astype(jnp.float32)[:, None] * freqs[None, :]
    return jnp.concatenate([jnp.cos(angles), jnp.sin(angles)], axis=1)


def group_sums(tensor, groups):
    batch_n, height_n, width_n, channels = tensor.shape
    split = tensor.reshape(batch_n, height_n, width_n, groups, channels // groups)
    return (jnp.sum(split, axis=(1, 2, 4)), jnp.sum(split * split, axis=(1, 2, 4)))


def spread(values, channels):
    return jnp.repeat(values, channels // values.shape[1], axis=1)[:, None, None, :]


def normalize(tensor, first_sum, square_sum, gains, scales, shifts, cell_count):
    channels = tensor.shape[3]
    average = first_sum / cell_count
    inverse = lax.rsqrt(square_sum / cell_count - average * average + EPS)
    normed = (tensor - spread(average, channels)) * spread(inverse, channels) * gains
    return normed * (1.0 + scales[:, None, None, :]) + shifts[:, None, None, :]


def patches(padded, height_n, width_n):
    return jnp.concatenate(
        [
            padded[:, vertical : vertical + height_n, lateral : lateral + width_n, :]
            for vertical in range(3)
            for lateral in range(3)
        ],
        axis=3,
    )


def convolve(padded, matrix):
    batch_n, height_p, width_p, channels = padded.shape
    flat = patches(padded, height_p - 2, width_p - 2).reshape(-1, 9 * channels)
    return jnp.dot(flat, matrix, preferred_element_type=jnp.float32).reshape(
        batch_n, height_p - 2, width_p - 2, matrix.shape[1]
    )


def flip_weight(weight):
    channels = weight.shape[2]
    return jnp.transpose(weight[::-1, ::-1], (0, 1, 3, 2)).reshape(9 * channels, channels)


def silu_slope(pre_act):
    sigmoid_v = jax.nn.sigmoid(pre_act)
    return sigmoid_v * (1.0 + pre_act * (1.0 - sigmoid_v))


def pad_columns(tensor):
    return jnp.pad(tensor, ((0, 0), (0, 0), (1, 1), (0, 0)))


def pick(stacked, index):
    return lax.dynamic_index_in_dim(stacked, index, 0, keepdims=False)


def norm_backward(tensor, first_sum, square_sum, gains, scales, shifts, cell_count, d_pre):

    def mapping(tensor_v, first_v, square_v, gains_v, scales_v, shifts_v):
        return normalize(tensor_v, first_v, square_v, gains_v, scales_v, shifts_v, cell_count)

    _, pull_back = jax.vjp(mapping, tensor, first_sum, square_sum, gains, scales, shifts)
    return pull_back(d_pre)


def per_device(images, steps, out_grad, conv_weight, gn_gain, emb_weight):
    section_count = lax.axis_size("section")
    tick_count = MICRO + section_count - 1
    section_no = lax.axis_index("section")
    local_n = images.shape[0] // MICRO
    row_count = images.shape[1]
    col_count = images.shape[2]
    channels = images.shape[3]
    cell_count = row_count * lax.axis_size("space") * col_count * (channels // G)
    weight = conv_weight[0]
    flat_weight = weight.reshape(9 * channels, channels)
    flipped = flip_weight(weight)
    gains = gn_gain[0]
    all_features = sinusoid(steps, FREQ)
    features = all_features.reshape(MICRO, local_n, FREQ)
    embedded = jnp.dot(
        all_features, emb_weight[0].astype(jnp.float32), precision=lax.Precision.HIGHEST
    ).reshape(MICRO, local_n, 2 * channels)
    batches = images.reshape(MICRO, local_n, row_count, col_count, channels)
    cotangents = out_grad.reshape(MICRO, local_n, row_count, col_count, channels)
    blank = jnp.zeros((local_n, row_count, col_count, channels), jnp.bfloat16)
    carried = blank
    skips = []
    kept_in = []
    kept_first = []
    kept_square = []
    kept_pad = []
    for moment in range(tick_count):
        arrived = blank
        if moment > 0:
            arrived = from_behind(carried, "section", 1)
        inputs = jnp.where(section_no == 0, batches[min(moment, MICRO - 1)], arrived)
        late = moment - (section_count - 1)
        if 0 <= late < MICRO:
            joined = (arrived.astype(jnp.float32) + skips[late].astype(jnp.float32)).astype(
                jnp.bfloat16
            )
            inputs = jnp.where(section_no == section_count - 1, joined, inputs)
        which = jnp.clip(moment - section_no, 0, MICRO - 1)
        chosen = pick(embedded, which)
        tensor = inputs.astype(jnp.float32)
        first_sum, square_sum = group_sums(tensor, G)
        first_sum, square_sum = lax.psum((first_sum, square_sum), "space")
        pre_act = normalize(
            tensor,
            first_sum,
            square_sum,
            gains,
            chosen[:, :channels],
            chosen[:, channels:],
            cell_count,
        )
        activation = jax.nn.silu(pre_act).astype(jnp.bfloat16)
        padded = pad_columns(extended(activation, (("space", 1),), 1))
        conv_out = convolve(padded, flat_weight)
        output = (tensor + conv_out).astype(jnp.bfloat16)
        if moment < MICRO:
            skips.append(from_behind(output, "section", section_count - 1))
        kept_in.append(inputs)
        kept_first.append(first_sum)
        kept_square.append(square_sum)
        kept_pad.append(padded)
        carried = output
    stack_in = jnp.stack(kept_in)
    stack_first = jnp.stack(kept_first)
    stack_square = jnp.stack(kept_square)
    stack_pad = jnp.stack(kept_pad)
    weight_grad = jnp.zeros((9 * channels, channels), jnp.float32)
    gain_grad = jnp.zeros((channels,), jnp.float32)
    emb_grad = jnp.zeros((FREQ, 2 * channels), jnp.float32)
    carried = blank
    skip_grads = []
    for moment in range(tick_count):
        arrived = blank
        if moment > 0:
            arrived = from_behind(carried, "section", -1)
        top_grad = cotangents[moment] if moment < MICRO else blank
        upstream = jnp.where(section_no == section_count - 1, top_grad, arrived)
        early = moment - (section_count - 1)
        if 0 <= early < MICRO:
            joined = (arrived.astype(jnp.float32) + skip_grads[early].astype(jnp.float32)).astype(
                jnp.bfloat16
            )
            upstream = jnp.where(section_no == 0, joined, upstream)
        which_raw = moment - (section_count - 1) + section_no
        valid = (which_raw >= 0) & (which_raw < MICRO)
        upstream = jnp.where(valid, upstream, blank)
        which = jnp.clip(which_raw, 0, MICRO - 1)
        forward_at = jnp.clip(which_raw + section_no, 0, tick_count - 1)
        tensor = pick(stack_in, forward_at).astype(jnp.float32)
        first_sum = pick(stack_first, forward_at)
        square_sum = pick(stack_square, forward_at)
        chosen = pick(embedded, which)
        scales = chosen[:, :channels]
        shifts = chosen[:, channels:]
        pre_act = normalize(tensor, first_sum, square_sum, gains, scales, shifts, cell_count)
        padded = pick(stack_pad, forward_at)
        flat_patch = patches(padded, row_count, col_count).reshape(-1, 9 * channels)
        weight_grad = weight_grad + jnp.dot(
            flat_patch.T, upstream.reshape(-1, channels), preferred_element_type=jnp.float32
        )
        up_pad = pad_columns(extended(upstream, (("space", 1),), 1))
        d_act = convolve(up_pad, flipped)
        d_pre = d_act * silu_slope(pre_act)
        d_tensor, d_first, d_square, d_gains, d_scales, d_shifts = norm_backward(
            tensor, first_sum, square_sum, gains, scales, shifts, cell_count, d_pre
        )
        d_first, d_square = lax.psum((d_first, d_square), "space")
        d_tensor = d_tensor + spread(d_first, channels) + 2.0 * tensor * spread(d_square, channels)
        d_input = (upstream.astype(jnp.float32) + d_tensor).astype(jnp.bfloat16)
        gain_grad = gain_grad + d_gains
        emb_grad = emb_grad + jnp.dot(
            pick(features, which).T,
            jnp.concatenate([d_scales, d_shifts], axis=1),
            precision=lax.Precision.HIGHEST,
        )
        if moment < MICRO:
            skip_grads.append(from_behind(d_input, "section", -(section_count - 1)))
        carried = d_input
    grads = (weight_grad.reshape(1, 3, 3, channels, channels), gain_grad[None], emb_grad[None])
    totals = lax.psum((grads[0], grads[1], grads[2]), ("dp", "space"))
    return (totals[0], totals[1], totals[2])


def solution(mesh):
    in_specs = (
        P("dp", "space", None, None),
        P("dp"),
        P("dp", "space", None, None),
        P("section", None, None, None, None),
        P("section", None),
        P("section", None, None),
    )
    out_specs = (P("section", None, None, None, None), P("section", None), P("section", None, None))
    return jax.shard_map(
        per_device, mesh=mesh, in_specs=in_specs, out_specs=out_specs, check_vma=False
    )
```

profile of v0, /device:TPU:32, one launch (start us, length us, event | category | flops | bytes accessed | tf_op | source)
XLA Modules:
  0.0 1326.5 jit_solution(16995887459301476496)
XLA Ops:
  9.3 3.0 collective-permute-start.16
  14.3 7.7 all-reduce.19
  24.2 1.3 collective-permute-start.1
  25.5 3.0 collective-permute-start
  28.6 1.4 constant_dynamic-update-slice_fusion.72
  30.6 1.6 copy.9
  34.2 10.0 collective-permute-start.9
  52.3 6.5 all-reduce.18
  59.2 1.3 collective-permute-start.4
  60.5 3.0 collective-permute-start.3
  65.0 1.6 collective-permute-start.13
  67.9 1.5 collective-permute-done.5
  70.5 7.2 all-reduce.17
  78.1 1.3 collective-permute-start.7
  79.4 3.0 collective-permute-start.6
  83.8 5.1 collective-permute-start.8
  89.0 1.5 collective-permute-done.8
  91.6 7.8 all-reduce.16
  100.3 1.3 collective-permute-start.11
  101.6 3.0 collective-permute-start.10
  106.8 5.8 collective-permute-start.12
  115.2 7.8 all-reduce.15
  124.7 1.4 fusion.60
  126.5 7.2 all-reduce.14
  134.1 1.3 collective-permute-start.18
  135.5 7.2 collective-permute-done.18
  142.6 1.3 collective-permute-start.20
  143.9 3.0 collective-permute-start.19
  147.0 1.3 collective-permute-start.25
  149.7 6.1 all-reduce.13
  156.1 1.3 collective-permute-start.21
  157.4 6.3 collective-permute-done.21
  165.1 3.0 collective-permute-start.22
  170.0 1.3 collective-permute-start.29
  172.4 7.5 all-reduce.12
  180.3 1.3 collective-permute-start.24
  181.7 6.2 collective-permute-done.24
  187.9 1.3 collective-permute-start.27
  189.2 3.0 collective-permute-start.26
  194.1 6.9 all-reduce.11
  201.4 1.3 collective-permute-start.15
  202.7 3.0 collective-permute-start.14
  207.1 6.6 collective-permute-done.28
  215.0 3.6 collective-permute-start.30
  221.6 1.9 convolution_add_fusion
  225.3 279.0 %psum.178 = f32[1,256]{1,0:T(1,128)} all-reduce(f32[1,256]{1,0:T(1,128)S(1)} %bitcast.511), channel_id=1, replica_groups=mesh['dp'=32,'section'=4,'space'=4] {'dp','space'}, use_global_device_ids=true, to_apply=%region_60.61 | all-reduce | flops 256 | bytes 2048 | tf_op jit(solution)/shard_map/psum | solution.py:223
  504.3 811.3 %all-reduce.22.cloned.1.call-done = (f32[1,3,3,256,256]{4,3,2,1,0:T(8,128)}, f32[1,256,512]{2,1,0:T(8,128)}) async-done(((f32[1,3,3,256,256]{4,3,2,1,0:T(8,128)}, f32[1,256,512]{2,1,0:T(8,128)}), (f32[1,3,3,256,256]{4,3,2,1,0:T(8,128)}, f32[1,256,512]{2,1,0:T(8,128)})) %all-reduce.22.cloned.1.call-update) | async-done | bytes 2883600 | tf_op jit(solution)/shard_map/psum | solution.py:223
  1315.6 3.3 copy.140
  (400 shorter events, 47.6 us)
Async XLA Ops:
  7.2 15.3 %copy-start = (bf16[1,256,512]{2,1,0:T(8,128)(2,1)S(1)}, bf16[1,256,512]{2,1,0:T(8,128)(2,1)}, u32[]{:S(2)}) copy-start(bf16[1,256,512]{2,1,0:T(8,128)(2,1)} %param.11) | copy-start | bytes 786436
  7.2 1308.4 %all-reduce.22.cloned.1.call-start = ((), (), s32[]{:S(2)}) async-start(), calls=%async_computation | async-start | bytes 5767168 | tf_op jit(solution)/shard_map/psum | solution.py:223
  8.0 37.5 %collective-permute-start.17 = (bf16[1,1,64,256]{3,2,1,0:T(8,128)(2,1)S(1)}, bf16[1,1,64,256]{3,2,1,0:T(8,128)(2,1)S(1)}, u32[]{:S(2)}, u32[]{:S(2)}) collective-permute-start(bf16[1,1,64,256]{3,2,1,0:T(8,128)(2,1)S(1)} %select_select_fusion.2), channel_id=1, source_target_pairs={{1,0},{2,1},{3,2},{5,4},{6,5},{7,6},{9,8},{10,9},{11,10},{13,12},{... | collective-permute-start | bytes 98312 | tf_op jit(solution)/shard_map/ppermute | solution.py:27
  9.3 36.3 %collective-permute-start.16 = (bf16[1,1,64,256]{3,2,1,0:T(8,128)(2,1)S(1)}, bf16[1,1,64,256]{3,2,1,0:T(8,128)(2,1)S(1)}, u32[]{:S(2)}, u32[]{:S(2)}) collective-permute-start(bf16[1,1,64,256]{3,2,1,0:T(8,128)(2,1)S(1)} %select_select_fusion.2), channel_id=1, source_target_pairs={{0,1},{1,2},{2,3},{4,5},{5,6},{6,7},{8,9},{9,10},{10,11},{12,13},{... | collective-permute-start | bytes 98312 | tf_op jit(solution)/shard_map/ppermute | solution.py:26
  24.2 9.0 collective-permute-start.1
  25.5 7.7 collective-permute-start
  33.4 14.7 %copy-start.5 = (bf16[2,1,64,256]{3,2,1,0:T(8,128)(2,1)S(1)}, bf16[2,1,64,256]{3,2,1,0:T(8,128)(2,1)}, u32[]{:S(2)}) copy-start(bf16[2,1,64,256]{3,2,1,0:T(8,128)(2,1)} %param.8) | copy-start | bytes 196612
  34.2 54.7 %collective-permute-start.9 = (bf16[1,1,64,256]{3,2,1,0:T(8,128)(2,1)S(1)}, bf16[1,1,64,256]{3,2,1,0:T(8,128)(2,1)S(1)}, u32[]{:S(2)}, u32[]{:S(2)}) collective-permute-start(bf16[1,1,64,256]{3,2,1,0:T(8,128)(2,1)S(1)} %fusion.8), channel_id=1, source_target_pairs={{0,12},{1,13},{2,14},{3,15},{16,28},{17,29},{18,30},{19,31},{32,44... | collective-permute-start | bytes 98312 | tf_op jit(solution)/shard_map/ppermute | solution.py:16
  44.3 7.0 collective-permute-start.2
  59.2 4.4 collective-permute-start.4
  60.5 3.9 collective-permute-start.3
  65.0 48.1 %collective-permute-start.13 = (bf16[1,1,64,256]{3,2,1,0:T(8,128)(2,1)S(1)}, bf16[1,1,64,256]{3,2,1,0:T(8,128)(2,1)S(1)}, u32[]{:S(2)}, u32[]{:S(2)}) collective-permute-start(bf16[1,1,64,256]{3,2,1,0:T(8,128)(2,1)S(1)} %fusion.6), channel_id=1, source_target_pairs={{0,12},{1,13},{2,14},{3,15},{16,28},{17,29},{18,30},{19,31},{32,44... | collective-permute-start | bytes 98312 | tf_op jit(solution)/shard_map/ppermute | solution.py:16
  66.6 2.9 collective-permute-start.5
  78.1 4.4 collective-permute-start.7
  79.4 3.9 collective-permute-start.6
  83.8 6.7 collective-permute-start.8
  100.3 12.3 copy-start.27
  100.3 4.4 collective-permute-start.11
  101.6 3.9 collective-permute-start.10
  105.6 19.1 %copy-start.3 = (bf16[3,3,256,256]{2,3,1,0:T(8,128)(2,1)S(1)}, bf16[3,3,256,256]{2,3,1,0:T(8,128)(2,1)}, u32[]{:S(2)}) copy-start(bf16[3,3,256,256]{2,3,1,0:T(8,128)(2,1)} %rev.3) | copy-start | bytes 3538948
  106.8 27.3 %copy-start.19 = (f32[1,256]{1,0:T(1,128)S(1)}, f32[1,256]{1,0:T(1,128)}, u32[]{:S(2)}) copy-start(f32[1,256]{1,0:T(1,128)} %get-tuple-element.96) | copy-start | bytes 3076
  106.8 7.3 collective-permute-start.12
  114.8 19.3 %copy-start.7 = (bf16[5,1,1,64,256]{4,3,2,1,0:T(8,128)(2,1)S(1)}, bf16[5,1,1,64,256]{4,3,2,1,0:T(8,128)(2,1)}, u32[]{:S(2)}) copy-start(bf16[5,1,1,64,256]{4,3,2,1,0:T(8,128)(2,1)} %get-tuple-element.70) | copy-start | bytes 491524
  124.6 24.2 %copy-start.18 = (f32[1,256]{1,0:T(1,128)S(1)}, f32[1,256]{1,0:T(1,128)}, u32[]{:S(2)}) copy-start(f32[1,256]{1,0:T(1,128)} %get-tuple-element.95) | copy-start | bytes 3076
  124.6 24.2 %copy-start.25 = (f32[1,256]{1,0:T(1,128)S(1)}, f32[1,256]{1,0:T(1,128)}, u32[]{:S(2)}) copy-start(f32[1,256]{1,0:T(1,128)} %get-tuple-element.105) | copy-start | bytes 3076
  134.1 8.5 collective-permute-start.18
  142.6 6.0 collective-permute-start.20
  143.9 4.7 collective-permute-start.19
  147.0 34.7 %collective-permute-start.25 = (bf16[1,1,64,256]{3,2,1,0:T(8,128)(2,1)S(1)}, bf16[1,1,64,256]{3,2,1,0:T(8,128)(2,1)S(1)}, u32[]{:S(2)}, u32[]{:S(2)}) collective-permute-start(bf16[1,1,64,256]{3,2,1,0:T(8,128)(2,1)S(1)} %fusion.123), channel_id=1, source_target_pairs={{12,0},{13,1},{14,2},{15,3},{28,16},{29,17},{30,18},{31,19},{44,32... | collective-permute-start | bytes 98312 | tf_op jit(solution)/shard_map/ppermute | solution.py:16
  148.8 22.7 %copy-start.17 = (f32[1,256]{1,0:T(1,128)S(1)}, f32[1,256]{1,0:T(1,128)}, u32[]{:S(2)}) copy-start(f32[1,256]{1,0:T(1,128)} %get-tuple-element.94) | copy-start | bytes 3076
  148.8 22.7 %copy-start.24 = (f32[1,256]{1,0:T(1,128)S(1)}, f32[1,256]{1,0:T(1,128)}, u32[]{:S(2)}) copy-start(f32[1,256]{1,0:T(1,128)} %get-tuple-element.104) | copy-start | bytes 3076
  156.1 7.6 collective-permute-start.21
  163.8 7.6 collective-permute-start.23
  165.1 6.3 collective-permute-start.22
  170.0 37.1 %collective-permute-start.29 = (bf16[1,1,64,256]{3,2,1,0:T(8,128)(2,1)S(1)}, bf16[1,1,64,256]{3,2,1,0:T(8,128)(2,1)S(1)}, u32[]{:S(2)}, u32[]{:S(2)}) collective-permute-start(bf16[1,1,64,256]{3,2,1,0:T(8,128)(2,1)S(1)} %fusion.75), channel_id=1, source_target_pairs={{12,0},{13,1},{14,2},{15,3},{28,16},{29,17},{30,18},{31,19},{44,32... | collective-permute-start | bytes 98312 | tf_op jit(solution)/shard_map/ppermute | solution.py:16
  171.6 21.7 %copy-start.14 = (f32[1,256]{1,0:T(1,128)S(1)}, f32[1,256]{1,0:T(1,128)}, u32[]{:S(2)}) copy-start(f32[1,256]{1,0:T(1,128)} %get-tuple-element.93) | copy-start | bytes 3076
  171.6 21.7 %copy-start.23 = (f32[1,256]{1,0:T(1,128)S(1)}, f32[1,256]{1,0:T(1,128)}, u32[]{:S(2)}) copy-start(f32[1,256]{1,0:T(1,128)} %get-tuple-element.103) | copy-start | bytes 3076
  180.3 7.5 collective-permute-start.24
  187.9 4.4 collective-permute-start.27
  189.2 3.9 collective-permute-start.26
  193.1 8.2 copy-start.15
  193.1 8.2 copy-start.16
  201.4 17.2 %collective-permute-start.15 = (bf16[1,1,64,256]{3,2,1,0:T(8,128)(2,1)S(1)}, bf16[1,1,64,256]{3,2,1,0:T(8,128)(2,1)S(1)}, u32[]{:S(2)}, u32[]{:S(2)}) collective-permute-start(bf16[1,1,64,256]{3,2,1,0:T(8,128)(2,1)S(1)} %get-tuple-element.118), channel_id=1, source_target_pairs={{1,0},{2,1},{3,2},{5,4},{6,5},{7,6},{9,8},{10,9},{11,10},{13,12},{... | collective-permute-start | bytes 98312 | tf_op jit(solution)/shard_map/ppermute | solution.py:27
  202.7 15.9 %collective-permute-start.14 = (bf16[1,1,64,256]{3,2,1,0:T(8,128)(2,1)S(1)}, bf16[1,1,64,256]{3,2,1,0:T(8,128)(2,1)S(1)}, u32[]{:S(2)}, u32[]{:S(2)}) collective-permute-start(bf16[1,1,64,256]{3,2,1,0:T(8,128)(2,1)S(1)} %get-tuple-element.118), channel_id=1, source_target_pairs={{0,1},{1,2},{2,3},{4,5},{5,6},{6,7},{8,9},{9,10},{10,11},{12,13},{... | collective-permute-start | bytes 98312 | tf_op jit(solution)/shard_map/ppermute | solution.py:26
  205.8 7.9 collective-permute-start.28
  213.7 9.8 collective-permute-start.31
  215.0 8.5 collective-permute-start.30
  1315.6 3.3 copy-start.4
  (13 other events, 14.1 us)
Sparse Core Ops, SparseCore 0:
  225.4 1090.1 all-reduce.21
where the time goes:
time: 1330 us
  waiting for transfers between devices  845 us (64%)
  blocking collectives  344 us (26%)
  starting transfers between devices  76.6 us (6%)
  local copies, waits for them, and re-layouts  20.9 us (2%)
  between operations  16.3 us (1%)
  other arithmetic  15.7 us (1%)
    psum x1, waiting for transfers between devices, per_device(): totals = lax.psum((grads[0], grads[1], grads[2]), ('dp', 'space'))  811 us
    psum x1, blocking collectives, per_device(): totals = lax.psum((grads[0], grads[1], grads[2]), ('dp', 'space'))  279 us
    psum x5, blocking collectives, per_device(): first_sum, square_sum = lax.psum((first_sum, square_sum), 'space')  36.9 us
    ppermute x12, starting transfers between devices, from_behind(): lax.ppermute(value, axis, [(source, source + steps) for source in range(i...  32.8 us
    ppermute x10, starting transfers between devices, extended(): before = lax.ppermute(last, axis, up)  30.9 us
    ppermute x12, waiting for transfers between devices, from_behind(): lax.ppermute(value, axis, [(source, source + steps) for source in range(i...  30.4 us
    psum x4, blocking collectives, per_device(): d_first, d_square = lax.psum((d_first, d_square), 'space')  27.7 us
  transfers between devices with their start and end apart: 33, of which 12 were waited for; matrix products, arithmetic and copies ran while one was open for 2% of the time, Pallas kernels for 0%

commit v1 on v0

--- a/solution.py
+++ b/solution.py
@@ -220,7 +220,7 @@
             skip_grads.append(from_behind(d_input, "section", -(section_count - 1)))
         carried = d_input
     grads = (weight_grad.reshape(1, 3, 3, channels, channels), gain_grad[None], emb_grad[None])
-    totals = lax.psum((grads[0], grads[1], grads[2]), ("dp", "space"))
+    totals = lax.psum(lax.psum((grads[0], grads[1], grads[2]), "dp"), "space")
     return (totals[0], totals[1], totals[2])
 
 

time: 1330 us -> 490 us (0.37)
  the two profiles are of different devices: /device:TPU:32 before, /device:TPU:1 now
where the time goes in v1:
time: 490 us; the launch traced here: 489 us
  waiting for transfers between devices  196 us (40%)
  blocking collectives  136 us (28%)
  starting transfers between devices  94.5 us (19%)
  local copies, waits for them, and re-layouts  20.9 us (4%)
  between operations  16.3 us (3%)
  other arithmetic  15.7 us (3%)
  matrix products  8.35 us (2%)
    psum x2, waiting for transfers between devices, per_device(): totals = lax.psum(lax.psum((grads[0], grads[1], grads[2]), 'dp'), 'space')  167 us
    psum x2, blocking collectives, per_device(): totals = lax.psum(lax.psum((grads[0], grads[1], grads[2]), 'dp'), 'space')  82.5 us
    ppermute x10, starting transfers between devices, extended(): after = lax.ppermute(initial, axis, down)  34.5 us
    ppermute x10, starting transfers between devices, extended(): before = lax.ppermute(last, axis, up)  31.7 us
    psum x5, blocking collectives, per_device(): first_sum, square_sum = lax.psum((first_sum, square_sum), 'space')  31.5 us
    ppermute x12, starting transfers between devices, from_behind(): lax.ppermute(value, axis, [(source, source + steps) for source in range(i...  28.2 us
    ppermute x12, waiting for transfers between devices, from_behind(): lax.ppermute(value, axis, [(source, source + steps) for source in range(i...  25.4 us
    psum x4, blocking collectives, per_device(): d_first, d_square = lax.psum((d_first, d_square), 'space')  22.4 us
  transfers between devices with their start and end apart: 34, of which 13 were waited for; matrix products, arithmetic and copies ran while one was open for 7% of the time, Pallas kernels for 0%

profile of v1, /device:TPU:1, one launch (start us, length us, event | category | flops | bytes accessed | tf_op | source)
XLA Modules:
  0.0 488.7 jit_solution(9658178572389038666)
XLA Ops:
  8.0 8.8 %collective-permute-start.17 = (bf16[1,1,64,256]{3,2,1,0:T(8,128)(2,1)S(1)}, bf16[1,1,64,256]{3,2,1,0:T(8,128)(2,1)S(1)}, u32[]{:S(2)}, u32[]{:S(2)}) collective-permute-start(bf16[1,1,64,256]{3,2,1,0:T(8,128)(2,1)S(1)} %select_select_fusion.2), channel_id=1, source_target_pairs={{1,0},{2,1},{3,2},{5,4},{6,5},{7,6},{9,8},{10,9},{11,10},{13,12},{... | collective-permute-start | bytes 98312 | tf_op jit(solution)/shard_map/ppermute | solution.py:27
  16.8 1.9 collective-permute-start.16
  20.7 5.5 %all-reduce.19 = (f32[1,32]{1,0:T(1,128)S(1)}, f32[1,32]{1,0:T(1,128)S(1)}) all-reduce(f32[1,32]{1,0:T(1,128)S(1)} %bitcast.533, f32[1,32]{1,0:T(1,128)S(1)} %bitcast.532), channel_id=1, replica_groups=mesh['dp'=32,'section'=4,'space'=4] {'space'}, use_global_device_ids=true, to_apply=%region_5.6 | all-reduce | flops 64 | bytes 512 | tf_op jit(solution)/shard_map/psum | solution.py:145
  28.4 2.7 collective-permute-start.1
  31.0 3.2 collective-permute-start
  34.2 1.4 constant_dynamic-update-slice_fusion.72
  36.2 1.6 copy.9
  39.9 6.3 %collective-permute-start.9 = (bf16[1,1,64,256]{3,2,1,0:T(8,128)(2,1)S(1)}, bf16[1,1,64,256]{3,2,1,0:T(8,128)(2,1)S(1)}, u32[]{:S(2)}, u32[]{:S(2)}) collective-permute-start(bf16[1,1,64,256]{3,2,1,0:T(8,128)(2,1)S(1)} %fusion.8), channel_id=1, source_target_pairs={{0,12},{1,13},{2,14},{3,15},{16,28},{17,29},{18,30},{19,31},{32,44... | collective-permute-start | bytes 98312 | tf_op jit(solution)/shard_map/ppermute | solution.py:16
  54.2 5.1 %all-reduce.18 = (f32[1,32]{1,0:T(1,128)S(1)}, f32[1,32]{1,0:T(1,128)S(1)}) all-reduce(f32[1,32]{1,0:T(1,128)S(1)} %bitcast.534, f32[1,32]{1,0:T(1,128)S(1)} %bitcast.528), channel_id=1, replica_groups=mesh['dp'=32,'section'=4,'space'=4] {'space'}, use_global_device_ids=true, to_apply=%region_11.12 | all-reduce | flops 64 | bytes 512 | tf_op jit(solution)/shard_map/psum | solution.py:145
  59.7 3.0 collective-permute-start.4
  62.7 3.2 collective-permute-start.3
  67.4 1.3 collective-permute-start.13
  72.0 7.0 %all-reduce.17 = (f32[1,32]{1,0:T(1,128)S(1)}, f32[1,32]{1,0:T(1,128)S(1)}) all-reduce(f32[1,32]{1,0:T(1,128)S(1)} %bitcast.535, f32[1,32]{1,0:T(1,128)S(1)} %bitcast.529), channel_id=1, replica_groups=mesh['dp'=32,'section'=4,'space'=4] {'space'}, use_global_device_ids=true, to_apply=%region_17.18 | all-reduce | flops 64 | bytes 512 | tf_op jit(solution)/shard_map/psum | solution.py:145
  79.4 2.1 collective-permute-start.7
  81.5 3.7 collective-permute-start.6
  86.8 4.8 collective-permute-start.8
  93.7 7.0 %all-reduce.16 = (f32[1,32]{1,0:T(1,128)S(1)}, f32[1,32]{1,0:T(1,128)S(1)}) all-reduce(f32[1,32]{1,0:T(1,128)S(1)} %bitcast.536, f32[1,32]{1,0:T(1,128)S(1)} %bitcast.530), channel_id=1, replica_groups=mesh['dp'=32,'section'=4,'space'=4] {'space'}, use_global_device_ids=true, to_apply=%region_23.24 | all-reduce | flops 64 | bytes 512 | tf_op jit(solution)/shard_map/psum | solution.py:145
  101.6 2.1 collective-permute-start.11
  103.7 3.7 collective-permute-start.10
  109.8 5.5 %collective-permute-start.12 = (bf16[1,1,64,256]{3,2,1,0:T(8,128)(2,1)S(1)}, bf16[1,1,64,256]{3,2,1,0:T(8,128)(2,1)S(1)}, u32[]{:S(2)}, u32[]{:S(2)}) collective-permute-start(bf16[1,1,64,256]{3,2,1,0:T(8,128)(2,1)S(1)} %fusion.4), channel_id=1, source_target_pairs={{0,4},{4,8},{8,12},{1,5},{5,9},{9,13},{2,6},{6,10},{10,14},{3,7},{... | collective-permute-start | bytes 98312 | tf_op jit(solution)/shard_map/ppermute | solution.py:16
  117.3 7.0 %all-reduce.15 = (f32[1,32]{1,0:T(1,128)S(1)}, f32[1,32]{1,0:T(1,128)S(1)}) all-reduce(f32[1,32]{1,0:T(1,128)S(1)} %bitcast.537, f32[1,32]{1,0:T(1,128)S(1)} %bitcast.531), channel_id=1, replica_groups=mesh['dp'=32,'section'=4,'space'=4] {'space'}, use_global_device_ids=true, to_apply=%region_29.30 | all-reduce | flops 64 | bytes 512 | tf_op jit(solution)/shard_map/psum | solution.py:145
  126.0 1.4 fusion.60
  127.8 5.8 %all-reduce.14 = (f32[1,32]{1,0:T(1,128)S(1)}, f32[32]{0:T(128)S(1)}) all-reduce(f32[1,32]{1,0:T(1,128)S(1)} %broadcast_multiply_fusion.3, f32[32]{0:T(128)S(1)} %get-tuple-element.70), channel_id=1, replica_groups=mesh['dp'=32,'section'=4,'space'=4] {'space'}, use_global_device_ids=true, to_apply=%region_35.36 | all-reduce | flops 64 | bytes 512 | tf_op jit(solution)/shard_map/psum | solution.py:210
  134.0 1.3 collective-permute-start.18
  135.3 5.9 %collective-permute-done.18 = bf16[1,1,64,256]{3,2,1,0:T(8,128)(2,1)S(1)} collective-permute-done((bf16[1,1,64,256]{3,2,1,0:T(8,128)(2,1)S(1)}, bf16[1,1,64,256]{3,2,1,0:T(8,128)(2,1)S(1)}, u32[]{:S(2)}, u32[]{:S(2)}) %collective-permute-start.18) | collective-permute-done | bytes 32800 | tf_op jit(solution)/shard_map/ppermute | solution.py:16
  141.3 4.8 collective-permute-start.20
  146.1 2.0 collective-permute-start.19
  148.1 1.3 collective-permute-start.25
  150.8 5.4 %all-reduce.13 = (f32[1,32]{1,0:T(1,128)S(1)}, f32[32]{0:T(128)S(1)}) all-reduce(f32[1,32]{1,0:T(1,128)S(1)} %broadcast_multiply_fusion.2, f32[32]{0:T(128)S(1)} %get-tuple-element.66), channel_id=1, replica_groups=mesh['dp'=32,'section'=4,'space'=4] {'space'}, use_global_device_ids=true, to_apply=%region_41.42 | all-reduce | flops 64 | bytes 512 | tf_op jit(solution)/shard_map/psum | solution.py:210
  157.9 6.2 %collective-permute-done.21 = bf16[1,1,64,256]{3,2,1,0:T(8,128)(2,1)S(1)} collective-permute-done((bf16[1,1,64,256]{3,2,1,0:T(8,128)(2,1)S(1)}, bf16[1,1,64,256]{3,2,1,0:T(8,128)(2,1)S(1)}, u32[]{:S(2)}, u32[]{:S(2)}) %collective-permute-start.21) | collective-permute-done | bytes 32800 | tf_op jit(solution)/shard_map/ppermute | solution.py:16
  164.2 3.0 collective-permute-start.23
  167.2 3.7 collective-permute-start.22
  175.2 5.1 %all-reduce.12 = (f32[1,32]{1,0:T(1,128)S(1)}, f32[32]{0:T(128)S(1)}) all-reduce(f32[1,32]{1,0:T(1,128)S(1)} %broadcast_multiply_fusion.1, f32[32]{0:T(128)S(1)} %get-tuple-element.62), channel_id=1, replica_groups=mesh['dp'=32,'section'=4,'space'=4] {'space'}, use_global_device_ids=true, to_apply=%region_47.48 | all-reduce | flops 64 | bytes 512 | tf_op jit(solution)/shard_map/psum | solution.py:210
  182.0 5.1 %collective-permute-done.24 = bf16[1,1,64,256]{3,2,1,0:T(8,128)(2,1)S(1)} collective-permute-done((bf16[1,1,64,256]{3,2,1,0:T(8,128)(2,1)S(1)}, bf16[1,1,64,256]{3,2,1,0:T(8,128)(2,1)S(1)}, u32[]{:S(2)}, u32[]{:S(2)}) %collective-permute-start.24) | collective-permute-done | bytes 32800 | tf_op jit(solution)/shard_map/ppermute | solution.py:16
  187.1 4.2 collective-permute-start.27
  191.3 2.8 collective-permute-start.26
  196.2 6.1 %all-reduce.11 = (f32[1,32]{1,0:T(1,128)S(1)}, f32[32]{0:T(128)S(1)}) all-reduce(f32[1,32]{1,0:T(1,128)S(1)} %broadcast_multiply_fusion, f32[32]{0:T(128)S(1)} %get-tuple-element.58), channel_id=1, replica_groups=mesh['dp'=32,'section'=4,'space'=4] {'space'}, use_global_device_ids=true, to_apply=%region_53.54 | all-reduce | flops 64 | bytes 512 | tf_op jit(solution)/shard_map/psum | solution.py:210
  202.7 2.1 collective-permute-start.15
  204.9 3.7 collective-permute-start.14
  209.9 5.7 %collective-permute-done.28 = bf16[1,1,64,256]{3,2,1,0:T(8,128)(2,1)S(1)} collective-permute-done((bf16[1,1,64,256]{3,2,1,0:T(8,128)(2,1)S(1)}, bf16[1,1,64,256]{3,2,1,0:T(8,128)(2,1)S(1)}, u32[]{:S(2)}, u32[]{:S(2)}) %collective-permute-start.28) | collective-permute-done | bytes 32800 | tf_op jit(solution)/shard_map/ppermute | solution.py:16
  215.6 1.9 collective-permute-start.31
  217.5 3.8 collective-permute-start.30
  224.4 1.9 convolution_add_fusion
  228.1 163.4 %all-reduce.24.cloned.1.call-done = (f32[1,3,3,256,256]{4,3,2,1,0:T(8,128)}, f32[1,256,512]{2,1,0:T(8,128)}) async-done(((f32[1,3,3,256,256]{4,3,2,1,0:T(8,128)}, f32[1,256,512]{2,1,0:T(8,128)}), (f32[1,3,3,256,256]{4,3,2,1,0:T(8,128)}, f32[1,256,512]{2,1,0:T(8,128)})) %all-reduce.24.cloned.1.call-update) | async-done | bytes 2883600 | tf_op jit(solution)/shard_map/psum | solution.py:223
  391.5 58.6 %psum.200 = f32[1,256]{1,0:T(1,128)S(1)} all-reduce(f32[1,256]{1,0:T(1,128)S(1)} %bitcast.511), channel_id=1, replica_groups=mesh['dp'=32,'section'=4,'space'=4] {'dp'}, use_global_device_ids=true, to_apply=%region_61.62 | all-reduce | flops 256 | bytes 2048 | tf_op jit(solution)/shard_map/psum | solution.py:223
  450.2 23.8 %psum.201 = f32[1,256]{1,0:T(1,128)} all-reduce(f32[1,256]{1,0:T(1,128)S(1)} %psum.200), channel_id=1, replica_groups=mesh['dp'=32,'section'=4,'space'=4] {'space'}, use_global_device_ids=true, to_apply=%region_62.63 | all-reduce | flops 256 | bytes 2048 | tf_op jit(solution)/shard_map/psum | solution.py:223
  474.0 3.7 all-reduce.26.cloned.1.call-done
  477.7 3.3 copy.142
  (404 shorter events, 49.7 us)
Async XLA Ops:
  7.2 19.5 %copy-start = (bf16[1,256,512]{2,1,0:T(8,128)(2,1)S(1)}, bf16[1,256,512]{2,1,0:T(8,128)(2,1)}, u32[]{:S(2)}) copy-start(bf16[1,256,512]{2,1,0:T(8,128)(2,1)} %param.11) | copy-start | bytes 786436
  7.2 384.3 %all-reduce.24.cloned.1.call-start = ((), (), s32[]{:S(2)}) async-start(), calls=%async_computation | async-start | bytes 5767168 | tf_op jit(solution)/shard_map/psum | solution.py:223
  8.0 39.4 %collective-permute-start.17 = (bf16[1,1,64,256]{3,2,1,0:T(8,128)(2,1)S(1)}, bf16[1,1,64,256]{3,2,1,0:T(8,128)(2,1)S(1)}, u32[]{:S(2)}, u32[]{:S(2)}) collective-permute-start(bf16[1,1,64,256]{3,2,1,0:T(8,128)(2,1)S(1)} %select_select_fusion.2), channel_id=1, source_target_pairs={{1,0},{2,1},{3,2},{5,4},{6,5},{7,6},{9,8},{10,9},{11,10},{13,12},{... | collective-permute-start | bytes 98312 | tf_op jit(solution)/shard_map/ppermute | solution.py:27
  16.8 30.6 %collective-permute-start.16 = (bf16[1,1,64,256]{3,2,1,0:T(8,128)(2,1)S(1)}, bf16[1,1,64,256]{3,2,1,0:T(8,128)(2,1)S(1)}, u32[]{:S(2)}, u32[]{:S(2)}) collective-permute-start(bf16[1,1,64,256]{3,2,1,0:T(8,128)(2,1)S(1)} %select_select_fusion.2), channel_id=1, source_target_pairs={{0,1},{1,2},{2,3},{4,5},{5,6},{6,7},{8,9},{9,10},{10,11},{12,13},{... | collective-permute-start | bytes 98312 | tf_op jit(solution)/shard_map/ppermute | solution.py:26
  28.4 10.5 %collective-permute-start.1 = (bf16[1,1,64,256]{3,2,1,0:T(8,128)(2,1)S(1)}, bf16[1,1,64,256]{3,2,1,0:T(8,128)(2,1)S(1)}, u32[]{:S(2)}, u32[]{:S(2)}) collective-permute-start(bf16[1,1,64,256]{3,2,1,0:T(8,128)(2,1)S(1)} %multiply_convert_fusion.4), channel_id=1, source_target_pairs={{1,0},{2,1},{3,2},{5,4},{6,5},{7,6},{9,8},{10,9},{11,10},{13,12},{... | collective-permute-start | bytes 98312 | tf_op jit(solution)/shard_map/ppermute | solution.py:27
  31.0 7.9 %collective-permute-start = (bf16[1,1,64,256]{3,2,1,0:T(8,128)(2,1)S(1)}, bf16[1,1,64,256]{3,2,1,0:T(8,128)(2,1)S(1)}, u32[]{:S(2)}, u32[]{:S(2)}) collective-permute-start(bf16[1,1,64,256]{3,2,1,0:T(8,128)(2,1)S(1)} %multiply_convert_fusion.4), channel_id=1, source_target_pairs={{0,1},{1,2},{2,3},{4,5},{5,6},{6,7},{8,9},{9,10},{10,11},{12,13},{... | collective-permute-start | bytes 98312 | tf_op jit(solution)/shard_map/ppermute | solution.py:26
  39.0 11.0 %copy-start.5 = (bf16[2,1,64,256]{3,2,1,0:T(8,128)(2,1)S(1)}, bf16[2,1,64,256]{3,2,1,0:T(8,128)(2,1)}, u32[]{:S(2)}) copy-start(bf16[2,1,64,256]{3,2,1,0:T(8,128)(2,1)} %param.8) | copy-start | bytes 196612
  39.9 51.8 %collective-permute-start.9 = (bf16[1,1,64,256]{3,2,1,0:T(8,128)(2,1)S(1)}, bf16[1,1,64,256]{3,2,1,0:T(8,128)(2,1)S(1)}, u32[]{:S(2)}, u32[]{:S(2)}) collective-permute-start(bf16[1,1,64,256]{3,2,1,0:T(8,128)(2,1)S(1)} %fusion.8), channel_id=1, source_target_pairs={{0,12},{1,13},{2,14},{3,15},{16,28},{17,29},{18,30},{19,31},{32,44... | collective-permute-start | bytes 98312 | tf_op jit(solution)/shard_map/ppermute | solution.py:16
  46.1 7.0 %collective-permute-start.2 = (bf16[1,1,64,256]{3,2,1,0:T(8,128)(2,1)S(1)}, bf16[1,1,64,256]{3,2,1,0:T(8,128)(2,1)S(1)}, u32[]{:S(2)}, u32[]{:S(2)}) collective-permute-start(bf16[1,1,64,256]{3,2,1,0:T(8,128)(2,1)S(1)} %fusion.8), channel_id=1, source_target_pairs={{0,4},{4,8},{8,12},{1,5},{5,9},{9,13},{2,6},{6,10},{10,14},{3,7},{... | collective-permute-start | bytes 98312 | tf_op jit(solution)/shard_map/ppermute | solution.py:16
  59.7 6.1 %collective-permute-start.4 = (bf16[1,1,64,256]{3,2,1,0:T(8,128)(2,1)S(1)}, bf16[1,1,64,256]{3,2,1,0:T(8,128)(2,1)S(1)}, u32[]{:S(2)}, u32[]{:S(2)}) collective-permute-start(bf16[1,1,64,256]{3,2,1,0:T(8,128)(2,1)S(1)} %multiply_convert_fusion.3), channel_id=1, source_target_pairs={{1,0},{2,1},{3,2},{5,4},{6,5},{7,6},{9,8},{10,9},{11,10},{13,12},{... | collective-permute-start | bytes 98312 | tf_op jit(solution)/shard_map/ppermute | solution.py:27
  62.7 4.2 collective-permute-start.3
  67.4 48.4 %collective-permute-start.13 = (bf16[1,1,64,256]{3,2,1,0:T(8,128)(2,1)S(1)}, bf16[1,1,64,256]{3,2,1,0:T(8,128)(2,1)S(1)}, u32[]{:S(2)}, u32[]{:S(2)}) collective-permute-start(bf16[1,1,64,256]{3,2,1,0:T(8,128)(2,1)S(1)} %fusion.6), channel_id=1, source_target_pairs={{0,12},{1,13},{2,14},{3,15},{16,28},{17,29},{18,30},{19,31},{32,44... | collective-permute-start | bytes 98312 | tf_op jit(solution)/shard_map/ppermute | solution.py:16
  68.7 2.3 collective-permute-start.5
  79.4 5.9 %collective-permute-start.7 = (bf16[1,1,64,256]{3,2,1,0:T(8,128)(2,1)S(1)}, bf16[1,1,64,256]{3,2,1,0:T(8,128)(2,1)S(1)}, u32[]{:S(2)}, u32[]{:S(2)}) collective-permute-start(bf16[1,1,64,256]{3,2,1,0:T(8,128)(2,1)S(1)} %multiply_convert_fusion.2), channel_id=1, source_target_pairs={{1,0},{2,1},{3,2},{5,4},{6,5},{7,6},{9,8},{10,9},{11,10},{13,12},{... | collective-permute-start | bytes 98312 | tf_op jit(solution)/shard_map/ppermute | solution.py:27
  81.5 4.7 collective-permute-start.6
  86.8 5.9 %collective-permute-start.8 = (bf16[1,1,64,256]{3,2,1,0:T(8,128)(2,1)S(1)}, bf16[1,1,64,256]{3,2,1,0:T(8,128)(2,1)S(1)}, u32[]{:S(2)}, u32[]{:S(2)}) collective-permute-start(bf16[1,1,64,256]{3,2,1,0:T(8,128)(2,1)S(1)} %fusion.5), channel_id=1, source_target_pairs={{0,4},{4,8},{8,12},{1,5},{5,9},{9,13},{2,6},{6,10},{10,14},{3,7},{... | collective-permute-start | bytes 98312 | tf_op jit(solution)/shard_map/ppermute | solution.py:16
  101.6 13.6 %copy-start.27 = (f32[1,32]{1,0:T(1,128)S(1)}, f32[1,32]{1,0:T(1,128)}, u32[]{:S(2)}) copy-start(f32[1,32]{1,0:T(1,128)} %copy-done.26) | copy-start | bytes 388
  101.6 5.8 %collective-permute-start.11 = (bf16[1,1,64,256]{3,2,1,0:T(8,128)(2,1)S(1)}, bf16[1,1,64,256]{3,2,1,0:T(8,128)(2,1)S(1)}, u32[]{:S(2)}, u32[]{:S(2)}) collective-permute-start(bf16[1,1,64,256]{3,2,1,0:T(8,128)(2,1)S(1)} %multiply_convert_fusion.1), channel_id=1, source_target_pairs={{1,0},{2,1},{3,2},{5,4},{6,5},{7,6},{9,8},{10,9},{11,10},{13,12},{... | collective-permute-start | bytes 98312 | tf_op jit(solution)/shard_map/ppermute | solution.py:27
  103.7 4.7 collective-permute-start.10
  108.5 17.4 %copy-start.3 = (bf16[3,3,256,256]{2,3,1,0:T(8,128)(2,1)S(1)}, bf16[3,3,256,256]{2,3,1,0:T(8,128)(2,1)}, u32[]{:S(2)}) copy-start(bf16[3,3,256,256]{2,3,1,0:T(8,128)(2,1)} %rev.3) | copy-start | bytes 3538948
  109.8 24.1 %copy-start.19 = (f32[1,256]{1,0:T(1,128)S(1)}, f32[1,256]{1,0:T(1,128)}, u32[]{:S(2)}) copy-start(f32[1,256]{1,0:T(1,128)} %get-tuple-element.98) | copy-start | bytes 3076
  109.8 6.5 %collective-permute-start.12 = (bf16[1,1,64,256]{3,2,1,0:T(8,128)(2,1)S(1)}, bf16[1,1,64,256]{3,2,1,0:T(8,128)(2,1)S(1)}, u32[]{:S(2)}, u32[]{:S(2)}) collective-permute-start(bf16[1,1,64,256]{3,2,1,0:T(8,128)(2,1)S(1)} %fusion.4), channel_id=1, source_target_pairs={{0,4},{4,8},{8,12},{1,5},{5,9},{9,13},{2,6},{6,10},{10,14},{3,7},{... | collective-permute-start | bytes 98312 | tf_op jit(solution)/shard_map/ppermute | solution.py:16
  116.9 17.0 %copy-start.7 = (bf16[5,1,1,64,256]{4,3,2,1,0:T(8,128)(2,1)S(1)}, bf16[5,1,1,64,256]{4,3,2,1,0:T(8,128)(2,1)}, u32[]{:S(2)}) copy-start(bf16[5,1,1,64,256]{4,3,2,1,0:T(8,128)(2,1)} %get-tuple-element.72) | copy-start | bytes 491524
  126.0 24.0 %copy-start.18 = (f32[1,256]{1,0:T(1,128)S(1)}, f32[1,256]{1,0:T(1,128)}, u32[]{:S(2)}) copy-start(f32[1,256]{1,0:T(1,128)} %get-tuple-element.97) | copy-start | bytes 3076
  126.0 24.0 %copy-start.25 = (f32[1,256]{1,0:T(1,128)S(1)}, f32[1,256]{1,0:T(1,128)}, u32[]{:S(2)}) copy-start(f32[1,256]{1,0:T(1,128)} %get-tuple-element.107) | copy-start | bytes 3076
  134.0 7.3 %collective-permute-start.18 = (bf16[1,1,64,256]{3,2,1,0:T(8,128)(2,1)S(1)}, bf16[1,1,64,256]{3,2,1,0:T(8,128)(2,1)S(1)}, u32[]{:S(2)}, u32[]{:S(2)}) collective-permute-start(bf16[1,1,64,256]{3,2,1,0:T(8,128)(2,1)S(1)} %fusion.123), channel_id=1, source_target_pairs={{4,0},{8,4},{12,8},{5,1},{9,5},{13,9},{6,2},{10,6},{14,10},{7,3},{... | collective-permute-start | bytes 98312 | tf_op jit(solution)/shard_map/ppermute | solution.py:16
  141.3 8.4 %collective-permute-start.20 = (bf16[1,1,64,256]{3,2,1,0:T(8,128)(2,1)S(1)}, bf16[1,1,64,256]{3,2,1,0:T(8,128)(2,1)S(1)}, u32[]{:S(2)}, u32[]{:S(2)}) collective-permute-start(bf16[1,1,64,256]{3,2,1,0:T(8,128)(2,1)S(1)} %select_select_fusion.1), channel_id=1, source_target_pairs={{1,0},{2,1},{3,2},{5,4},{6,5},{7,6},{9,8},{10,9},{11,10},{13,12},{... | collective-permute-start | bytes 98312 | tf_op jit(solution)/shard_map/ppermute | solution.py:27
  146.1 3.7 collective-permute-start.19
  148.1 33.9 %collective-permute-start.25 = (bf16[1,1,64,256]{3,2,1,0:T(8,128)(2,1)S(1)}, bf16[1,1,64,256]{3,2,1,0:T(8,128)(2,1)S(1)}, u32[]{:S(2)}, u32[]{:S(2)}) collective-permute-start(bf16[1,1,64,256]{3,2,1,0:T(8,128)(2,1)S(1)} %fusion.123), channel_id=1, source_target_pairs={{12,0},{13,1},{14,2},{15,3},{28,16},{29,17},{30,18},{31,19},{44,32... | collective-permute-start | bytes 98312 | tf_op jit(solution)/shard_map/ppermute | solution.py:16
  149.9 24.4 %copy-start.17 = (f32[1,256]{1,0:T(1,128)S(1)}, f32[1,256]{1,0:T(1,128)}, u32[]{:S(2)}) copy-start(f32[1,256]{1,0:T(1,128)} %get-tuple-element.96) | copy-start | bytes 3076
  150.0 24.4 %copy-start.24 = (f32[1,256]{1,0:T(1,128)S(1)}, f32[1,256]{1,0:T(1,128)}, u32[]{:S(2)}) copy-start(f32[1,256]{1,0:T(1,128)} %get-tuple-element.106) | copy-start | bytes 3076
  156.6 7.6 %collective-permute-start.21 = (bf16[1,1,64,256]{3,2,1,0:T(8,128)(2,1)S(1)}, bf16[1,1,64,256]{3,2,1,0:T(8,128)(2,1)S(1)}, u32[]{:S(2)}, u32[]{:S(2)}) collective-permute-start(bf16[1,1,64,256]{3,2,1,0:T(8,128)(2,1)S(1)} %fusion.75), channel_id=1, source_target_pairs={{4,0},{8,4},{12,8},{5,1},{9,5},{13,9},{6,2},{10,6},{14,10},{7,3},{... | collective-permute-start | bytes 98312 | tf_op jit(solution)/shard_map/ppermute | solution.py:16
  164.2 9.9 %collective-permute-start.23 = (bf16[1,1,64,256]{3,2,1,0:T(8,128)(2,1)S(1)}, bf16[1,1,64,256]{3,2,1,0:T(8,128)(2,1)S(1)}, u32[]{:S(2)}, u32[]{:S(2)}) collective-permute-start(bf16[1,1,64,256]{3,2,1,0:T(8,128)(2,1)S(1)} %select_select_fusion), channel_id=1, source_target_pairs={{1,0},{2,1},{3,2},{5,4},{6,5},{7,6},{9,8},{10,9},{11,10},{13,12},{... | collective-permute-start | bytes 98312 | tf_op jit(solution)/shard_map/ppermute | solution.py:27
  167.2 6.9 %collective-permute-start.22 = (bf16[1,1,64,256]{3,2,1,0:T(8,128)(2,1)S(1)}, bf16[1,1,64,256]{3,2,1,0:T(8,128)(2,1)S(1)}, u32[]{:S(2)}, u32[]{:S(2)}) collective-permute-start(bf16[1,1,64,256]{3,2,1,0:T(8,128)(2,1)S(1)} %select_select_fusion), channel_id=1, source_target_pairs={{0,1},{1,2},{2,3},{4,5},{5,6},{6,7},{8,9},{9,10},{10,11},{12,13},{... | collective-permute-start | bytes 98312 | tf_op jit(solution)/shard_map/ppermute | solution.py:26
  172.8 37.1 %collective-permute-start.29 = (bf16[1,1,64,256]{3,2,1,0:T(8,128)(2,1)S(1)}, bf16[1,1,64,256]{3,2,1,0:T(8,128)(2,1)S(1)}, u32[]{:S(2)}, u32[]{:S(2)}) collective-permute-start(bf16[1,1,64,256]{3,2,1,0:T(8,128)(2,1)S(1)} %fusion.75), channel_id=1, source_target_pairs={{12,0},{13,1},{14,2},{15,3},{28,16},{29,17},{30,18},{31,19},{44,32... | collective-permute-start | bytes 98312 | tf_op jit(solution)/shard_map/ppermute | solution.py:16
  174.3 21.0 %copy-start.14 = (f32[1,256]{1,0:T(1,128)S(1)}, f32[1,256]{1,0:T(1,128)}, u32[]{:S(2)}) copy-start(f32[1,256]{1,0:T(1,128)} %get-tuple-element.95) | copy-start | bytes 3076
  174.3 21.0 %copy-start.23 = (f32[1,256]{1,0:T(1,128)S(1)}, f32[1,256]{1,0:T(1,128)}, u32[]{:S(2)}) copy-start(f32[1,256]{1,0:T(1,128)} %get-tuple-element.105) | copy-start | bytes 3076
  180.7 6.4 %collective-permute-start.24 = (bf16[1,1,64,256]{3,2,1,0:T(8,128)(2,1)S(1)}, bf16[1,1,64,256]{3,2,1,0:T(8,128)(2,1)S(1)}, u32[]{:S(2)}, u32[]{:S(2)}) collective-permute-start(bf16[1,1,64,256]{3,2,1,0:T(8,128)(2,1)S(1)} %fusion.79), channel_id=1, source_target_pairs={{4,0},{8,4},{12,8},{5,1},{9,5},{13,9},{6,2},{10,6},{14,10},{7,3},{... | collective-permute-start | bytes 98312 | tf_op jit(solution)/shard_map/ppermute | solution.py:16
  187.1 7.0 %collective-permute-start.27 = (bf16[1,1,64,256]{3,2,1,0:T(8,128)(2,1)S(1)}, bf16[1,1,64,256]{3,2,1,0:T(8,128)(2,1)S(1)}, u32[]{:S(2)}, u32[]{:S(2)}) collective-permute-start(bf16[1,1,64,256]{3,2,1,0:T(8,128)(2,1)S(1)} %fusion.120), channel_id=1, source_target_pairs={{1,0},{2,1},{3,2},{5,4},{6,5},{7,6},{9,8},{10,9},{11,10},{13,12},{... | collective-permute-start | bytes 98312 | tf_op jit(solution)/shard_map/ppermute | solution.py:27
  191.3 3.8 collective-permute-start.26
  195.2 7.4 %copy-start.15 = (f32[1,256]{1,0:T(1,128)S(1)}, f32[1,256]{1,0:T(1,128)}, u32[]{:S(2)}) copy-start(f32[1,256]{1,0:T(1,128)} %get-tuple-element.99) | copy-start | bytes 3076
  195.2 7.4 %copy-start.16 = (f32[1,256]{1,0:T(1,128)S(1)}, f32[1,256]{1,0:T(1,128)}, u32[]{:S(2)}) copy-start(f32[1,256]{1,0:T(1,128)} %get-tuple-element.109) | copy-start | bytes 3076
  202.7 18.7 %collective-permute-start.15 = (bf16[1,1,64,256]{3,2,1,0:T(8,128)(2,1)S(1)}, bf16[1,1,64,256]{3,2,1,0:T(8,128)(2,1)S(1)}, u32[]{:S(2)}, u32[]{:S(2)}) collective-permute-start(bf16[1,1,64,256]{3,2,1,0:T(8,128)(2,1)S(1)} %get-tuple-element.120), channel_id=1, source_target_pairs={{1,0},{2,1},{3,2},{5,4},{6,5},{7,6},{9,8},{10,9},{11,10},{13,12},{... | collective-permute-start | bytes 98312 | tf_op jit(solution)/shard_map/ppermute | solution.py:27
  204.9 16.5 %collective-permute-start.14 = (bf16[1,1,64,256]{3,2,1,0:T(8,128)(2,1)S(1)}, bf16[1,1,64,256]{3,2,1,0:T(8,128)(2,1)S(1)}, u32[]{:S(2)}, u32[]{:S(2)}) collective-permute-start(bf16[1,1,64,256]{3,2,1,0:T(8,128)(2,1)S(1)} %get-tuple-element.120), channel_id=1, source_target_pairs={{0,1},{1,2},{2,3},{4,5},{5,6},{6,7},{8,9},{9,10},{10,11},{12,13},{... | collective-permute-start | bytes 98312 | tf_op jit(solution)/shard_map/ppermute | solution.py:26
  208.5 7.0 %collective-permute-start.28 = (bf16[1,1,64,256]{3,2,1,0:T(8,128)(2,1)S(1)}, bf16[1,1,64,256]{3,2,1,0:T(8,128)(2,1)S(1)}, u32[]{:S(2)}, u32[]{:S(2)}) collective-permute-start(bf16[1,1,64,256]{3,2,1,0:T(8,128)(2,1)S(1)} %get-tuple-element.119), channel_id=1, source_target_pairs={{4,0},{8,4},{12,8},{5,1},{9,5},{13,9},{6,2},{10,6},{14,10},{7,3},{... | collective-permute-start | bytes 98312 | tf_op jit(solution)/shard_map/ppermute | solution.py:16
  215.6 10.7 %collective-permute-start.31 = (bf16[1,1,64,256]{3,2,1,0:T(8,128)(2,1)S(1)}, bf16[1,1,64,256]{3,2,1,0:T(8,128)(2,1)S(1)}, u32[]{:S(2)}, u32[]{:S(2)}) collective-permute-start(bf16[1,1,64,256]{3,2,1,0:T(8,128)(2,1)S(1)} %fusion.122), channel_id=1, source_target_pairs={{1,0},{2,1},{3,2},{5,4},{6,5},{7,6},{9,8},{10,9},{11,10},{13,12},{... | collective-permute-start | bytes 98312 | tf_op jit(solution)/shard_map/ppermute | solution.py:27
  217.5 8.8 %collective-permute-start.30 = (bf16[1,1,64,256]{3,2,1,0:T(8,128)(2,1)S(1)}, bf16[1,1,64,256]{3,2,1,0:T(8,128)(2,1)S(1)}, u32[]{:S(2)}, u32[]{:S(2)}) collective-permute-start(bf16[1,1,64,256]{3,2,1,0:T(8,128)(2,1)S(1)} %fusion.122), channel_id=1, source_target_pairs={{0,1},{1,2},{2,3},{4,5},{5,6},{6,7},{8,9},{9,10},{10,11},{12,13},{... | collective-permute-start | bytes 98312 | tf_op jit(solution)/shard_map/ppermute | solution.py:26
  228.0 249.7 %all-reduce.26.cloned.1.call-start = ((), (), s32[]{:S(2)}) async-start(), calls=%async_computation.1 | async-start | bytes 5767168 | tf_op jit(solution)/shard_map/psum | solution.py:223
  (14 other events, 17.5 us)
Sparse Core Ops, SparseCore 0:
  228.2 163.2 all-reduce.23
  394.8 82.8 all-reduce.25
